TPU v7x, 512 devices: a whole 4x4x16 slice. The times are simulated.
512 devices in a mesh: group: 32 (over y, z_lo, core), expert: 16 (over x, z_hi).
Axes of the slice: x: 4, y: 4, z: 16 (z_hi: 4, z_lo: 4; z = z_hi * 4 + z_lo), core: 2. Of those that a mesh axis runs over, the one named last changes fastest.
Arguments:
- tokens: bfloat16 [65536, 1536], P(('group', 'expert')), may hold values from -6 to 6
- gate_train: float32 [32, 1536, 512], P('expert', 'group'), may hold values from -0.15625 to 0.15625
- up_train: float32 [32, 1536, 512], P('expert', 'group'), may hold values from -0.15625 to 0.15625
- down_train: float32 [32, 512, 1536], P('expert', None, 'group'), may hold values from -0.25 to 0.25
- routes: int32 [65536, 6], P(('group', 'expert')), may hold values from 0 to 31, as said below
- route_scores: float32 [65536, 6], P(('group', 'expert')), may hold values from 0.05 to 1
- live: int32 [65536], P(('group', 'expert')), may hold values from 0 to 1
Outputs:
- moe_out: bfloat16 [65536, 1536], P(('group', 'expert'))
Inputs may be any that keep to these rules, and one draw needn't show every extreme that they name: `routes`: each row names 6 different experts; one expert, the same on every device, is named by at least 24 live rows among each device's 128 rows.
All inputs are finite; a program needn't handle non-finite values.
Results may differ from a plain program's by a relative error of at most 0.0075.
Values may be sent and summed in bfloat16 or wider, within the bound.
No kernel may reach another device: no remote copies, remote signals or barrier semaphores. Data moves between devices by JAX's collectives and lax.ppermute only.
A program may use at most 64 MiB of HBM per device.

v0:
```python
import jax
import jax.numpy as jnp
from jax import lax
from jax.sharding import PartitionSpec as P


def local(tokens, gate_train, up_train, down_train, routes, route_scores, live):
    local_experts = gate_train.shape[0]
    hidden_width = gate_train.shape[2]
    holders = lax.axis_size("expert")
    experts = local_experts * holders
    tok_dev, model_width = tokens.shape
    top_count = routes.shape[1]
    capacity = tok_dev * top_count // experts
    total_slots = experts * capacity
    route_share = route_scores / jnp.sum(route_scores, axis=1, keepdims=True)
    flat_route = routes.reshape(-1)
    flat_live = jnp.repeat(live, top_count)
    expert_ids = jnp.arange(experts, dtype=jnp.int32)
    onehot = ((flat_route[:, None] == expert_ids[None, :]) & (flat_live[:, None] > 0)).astype(
        jnp.int32
    )
    earlier = jnp.cumsum(onehot, axis=0) - onehot
    slot_index = jnp.sum(earlier * onehot, axis=1)
    kept_mask = (flat_live > 0) & (slot_index < capacity)
    target = jnp.where(kept_mask, flat_route * capacity + slot_index, total_slots)
    anchor = jnp.arange(tok_dev * top_count, dtype=jnp.int32) // top_count
    source_row = jnp.zeros((total_slots,), jnp.int32).at[target].set(anchor, mode="drop")
    filled = jnp.zeros((total_slots,), jnp.int32).at[target].set(1, mode="drop")
    outgoing = jnp.where(filled[:, None] > 0, tokens[source_row], jnp.zeros((), jnp.bfloat16))
    outgoing = outgoing.reshape(holders, local_experts * capacity, model_width)
    incoming = lax.all_to_all(outgoing, "expert", split_axis=0, concat_axis=0, tiled=True)
    incoming = incoming.reshape(holders, local_experts, capacity, model_width)
    gate_up_local = jnp.concatenate([gate_train, up_train], axis=2).astype(jnp.bfloat16)
    down_local = down_train.astype(jnp.bfloat16)
    gate_up_w, down_w = (
        lax.all_gather(gate_up_local, "group", axis=1, tiled=True),
        lax.all_gather(down_local, "group", axis=2, tiled=True),
    )
    gate_up = jnp.einsum("sjcd,jdf->sjcf", incoming, gate_up_w, preferred_element_type=jnp.float32)
    hidden = (jax.nn.silu(gate_up[..., :hidden_width]) * gate_up[..., hidden_width:]).astype(
        jnp.bfloat16
    )
    expert_out = jnp.einsum("sjcf,jfd->sjcd", hidden, down_w, preferred_element_type=jnp.float32)
    expert_rows = expert_out.astype(jnp.bfloat16).reshape(
        holders, local_experts * capacity, model_width
    )
    returned = lax.all_to_all(
        expert_rows, "expert", split_axis=0, concat_axis=0, tiled=True
    ).reshape(total_slots, model_width)
    picked = returned[jnp.minimum(target, total_slots - 1)]
    weight = jnp.where(kept_mask, route_share.reshape(-1), 0.0)
    combined = jnp.sum(
        picked.reshape(tok_dev, top_count, model_width).astype(jnp.float32)
        * weight.reshape(tok_dev, top_count, 1),
        axis=1,
    )
    return combined.astype(jnp.bfloat16)


def solution(mesh):
    in_specs = (
        P(("group", "expert"), None),
        P("expert", "group", None),
        P("expert", "group", None),
        P("expert", None, "group"),
        P(("group", "expert"), None),
        P(("group", "expert"), None),
        P(("group", "expert")),
    )
    out_specs = P(("group", "expert"), None)
    return jax.shard_map(local, mesh=mesh, in_specs=in_specs, out_specs=out_specs, check_vma=False)
```

profile of v0, /device:TPU:48, one launch (start us, length us, event | category | flops | bytes accessed | tf_op | source)
XLA Modules:
  0.0 405.2 jit_solution(16092670859250466878)
XLA Ops:
  6.5 0.0 copy-start
  6.5 0.0 all-gather.3.cloned.1.call-start
  6.5 1.0 convert.7
  7.5 0.9 convert.8
  8.5 0.7 pad_maximum_fusion
  9.2 0.0 all-gather.3.cloned.1.call-update
  9.2 0.7 broadcast_compare_fusion.2
  9.9 0.1 broadcast_in_dim.37.clone
  10.0 0.2 gt.41
  10.1 0.1 gt.40
  10.3 0.8 copy.18
  11.1 0.1 eq.29
  11.2 0.1 eq.25
  11.3 0.1 gt.39
  11.5 1.7 reduce-window.6
  13.2 0.3 slice_reduce_fusion
  13.5 0.7 broadcast_multiply_fusion
  14.2 0.1 copy.23
  14.3 0.1 mul.37
  14.5 0.1 fusion.17
  14.7 3.4 scatter_custom_fusion.1
  18.0 3.4 scatter_custom_fusion
  21.4 0.1 broadcast_in_dim.40
  21.6 0.0 copy-done
  21.6 2.9 gather_fusion
  24.5 1.6 broadcast_select_fusion
  26.1 0.0 copy-start.1
  26.1 16.9 %all-to-all-start = ((bf16[16,48,1536]{2,1,0:T(8,128)(2,1)}), bf16[16,48,1536]{2,1,0:T(8,128)(2,1)S(1)}, u32[]{:S(2)}, u32[]{:S(2)}) async-start(bf16[16,48,1536]{2,1,0:T(8,128)(2,1)} %broadcast_select_fusion), calls=%async_computation | async-start | bytes 4718592 | tf_op jit(solution)/shard_map/all_to_all | solution.py:32
  43.0 0.0 all-gather.5.cloned.1.call-start
  43.1 0.0 copy-done.1
  43.1 0.7 convert_element_type.32
  43.7 0.0 all-gather.5.cloned.1.call-update
  43.8 104.8 %all-to-all-done = bf16[16,48,1536]{2,1,0:T(8,128)(2,1)S(1)} async-done(((bf16[16,48,1536]{2,1,0:T(8,128)(2,1)}), bf16[16,48,1536]{2,1,0:T(8,128)(2,1)S(1)}, u32[]{:S(2)}, u32[]{:S(2)}) %all-to-all-start) | async-done | bytes 2359328 | tf_op jit(solution)/shard_map/all_to_all | solution.py:32
  148.6 32.2 %all-gather.3.cloned.1.call-done = bf16[2,1536,1024]{2,1,0:T(8,128)(2,1)} async-done(((bf16[2,48,1024]{2,1,0:T(8,128)(2,1)}), bf16[2,1536,1024]{2,1,0:T(8,128)(2,1)}) %all-gather.3.cloned.1.call-update) | async-done | bytes 6291472 | tf_op jit(solution)/shard_map/all_gather | solution.py:37
  180.8 7.0 %fusion.7 = f32[16,2,24,1024]{3,2,0,1:T(8,128)} fusion(bf16[16,2,24,1536]{3,2,1,0:T(8,128)(2,1)S(1)} %bitcast.45, bf16[2,1536,1024]{2,1,0:T(8,128)(2,1)} %all-gather.3.cloned.1.call-done), kind=kOutput, calls=%fused_computation.12 | convolution fusion | flops 2415919104 | bytes 11796480 | tf_op jit(solution)/shard_map/sjcd,jdf->sjcf/dot_general | solution.py:40
  187.9 62.0 %all-gather.5.cloned.1.call-done = bf16[2,512,1536]{1,2,0:T(8,128)(2,1)} async-done(((bf16[2,512,48]{1,2,0:T(8,128)(2,1)}), bf16[2,512,1536]{1,2,0:T(8,128)(2,1)}) %all-gather.5.cloned.1.call-update) | async-done | bytes 3145744 | tf_op jit(solution)/shard_map/all_gather | solution.py:38
  249.9 4.3 %fusion.3 = bf16[16,2,24,1536]{3,2,0,1:T(8,128)(2,1)S(1)} fusion(bf16[2,512,1536]{1,2,0:T(8,128)(2,1)} %all-gather.5.cloned.1.call-done, f32[16,2,24,1024]{3,2,0,1:T(8,128)} %fusion.7), kind=kOutput, calls=%fused_computation.9 | convolution fusion | flops 1211498496 | bytes 8650752 | tf_op jit(solution)/shard_map/sjcf,jfd->sjcd/dot_general | solution.py:44
  254.2 1.7 copy.25
  255.9 0.0 copy-start.2
  255.9 13.0 %all-to-all-start.1 = ((bf16[16,48,1536]{2,1,0:T(8,128)(2,1)}), bf16[16,48,1536]{2,1,0:T(8,128)(2,1)S(1)}, u32[]{:S(2)}, u32[]{:S(2)}) async-start(bf16[16,48,1536]{2,1,0:T(8,128)(2,1)} %bitcast.43), calls=%async_computation.1 | async-start | bytes 4718592 | tf_op jit(solution)/shard_map/all_to_all | solution.py:48
  268.9 0.2 lt.50
  269.1 0.1 copy.26
  269.1 0.0 copy-done.2
  269.2 0.1 copy.27
  269.3 114.2 %all-to-all-done.1 = bf16[16,48,1536]{2,1,0:T(8,128)(2,1)S(1)} async-done(((bf16[16,48,1536]{2,1,0:T(8,128)(2,1)}), bf16[16,48,1536]{2,1,0:T(8,128)(2,1)S(1)}, u32[]{:S(2)}, u32[]{:S(2)}) %all-to-all-start.1) | async-done | bytes 2359328 | tf_op jit(solution)/shard_map/all_to_all | solution.py:48
  383.6 3.9 gather_fusion.1
  387.4 5.0 %reshape.148 = f32[128,6,1536]{2,1,0:T(8,128)} reshape(bf16[768,1536]{1,0:T(8,128)(2,1)} %gather_fusion.1) | data formatting | bytes 7077888 | tf_op jit(solution)/shard_map/convert_element_type | solution.py:54
  392.4 5.9 %multiply_reduce_fusion = bf16[128,1536]{1,0:T(8,128)(2,1)} fusion(f32[128,6,1536]{2,1,0:T(8,128)} %reshape.148, f32[128,6]{1,0:T(8,128)S(1)} %copy.27), kind=kLoop, calls=%fused_computation.6 | loop fusion | flops 2162688 | bytes 5114880 | tf_op jit(solution)/shard_map/reduce_sum | solution.py:53
  (12 shorter events, 0.2 us)
Async XLA Ops:
  6.5 15.0 %copy-start = (bf16[128,1536]{1,0:T(8,128)(2,1)S(1)}, bf16[128,1536]{1,0:T(8,128)(2,1)}, u32[]{:S(2)}) copy-start(bf16[128,1536]{1,0:T(8,128)(2,1)} %param.7) | copy-start | bytes 1179652
  6.5 174.3 %all-gather.3.cloned.1.call-start = ((), (), s32[]{:S(2)}) async-start(), calls=%async_computation.2 | async-start | bytes 6488064 | tf_op jit(solution)/shard_map/all_gather | solution.py:37
  26.1 16.9 %copy-start.1 = (f32[2,512,48]{1,2,0:T(8,128)S(1)}, f32[2,512,48]{1,2,0:T(8,128)}, u32[]{:S(2)}) copy-start(f32[2,512,48]{1,2,0:T(8,128)} %param.10) | copy-start | bytes 589828
  26.1 122.5 %all-to-all-start = ((bf16[16,48,1536]{2,1,0:T(8,128)(2,1)}), bf16[16,48,1536]{2,1,0:T(8,128)(2,1)S(1)}, u32[]{:S(2)}, u32[]{:S(2)}) async-start(bf16[16,48,1536]{2,1,0:T(8,128)(2,1)} %broadcast_select_fusion), calls=%async_computation | async-start | bytes 4718592 | tf_op jit(solution)/shard_map/all_to_all | solution.py:32
  43.0 206.8 %all-gather.5.cloned.1.call-start = ((), (), s32[]{:S(2)}) async-start(), calls=%async_computation.3 | async-start | bytes 3244032 | tf_op jit(solution)/shard_map/all_gather | solution.py:38
  255.9 13.3 %copy-start.2 = (f32[128,6]{0,1:T(8,128)S(1)}, f32[128,6]{0,1:T(8,128)}, u32[]{:S(2)}) copy-start(f32[128,6]{0,1:T(8,128)} %param.12) | copy-start | bytes 9220
  255.9 127.7 %all-to-all-start.1 = ((bf16[16,48,1536]{2,1,0:T(8,128)(2,1)}), bf16[16,48,1536]{2,1,0:T(8,128)(2,1)S(1)}, u32[]{:S(2)}, u32[]{:S(2)}) async-start(bf16[16,48,1536]{2,1,0:T(8,128)(2,1)} %bitcast.43), calls=%async_computation.1 | async-start | bytes 4718592 | tf_op jit(solution)/shard_map/all_to_all | solution.py:48
Sparse Core Ops, SparseCore 0:
  9.4 171.3 all-gather.2
  182.9 66.8 all-gather.4
where the time goes:
time: 406 us; the launch traced here: 405 us
  waiting for transfers between devices  313 us (77%)
  starting transfers between devices  29.9 us (7%)
  local copies, waits for them, and re-layouts  22.8 us (6%)
  other arithmetic  14.2 us (3%)
  between operations  13.6 us (3%)
  matrix products  11.3 us (3%)
    all_to_all x1, waiting for transfers between devices, local(): lax.all_to_all(expert_rows, 'expert', split_axis=0, concat_axis=0, tiled=...  114 us
    all_to_all x1, waiting for transfers between devices, local(): lax.all_to_all(outgoing, 'expert', split_axis=0, concat_axis=0, tiled=True)  105 us
    all_gather x1, waiting for transfers between devices, local(): lax.all_gather(down_local, 'group', axis=2, tiled=True)  62 us
    all_gather x1, waiting for transfers between devices, local(): lax.all_gather(gate_up_local, 'group', axis=1, tiled=True)  32.2 us
    all_to_all x1, starting transfers between devices, local(): lax.all_to_all(outgoing, 'expert', split_axis=0, concat_axis=0, tiled=True)  16.9 us
    all_to_all x1, starting transfers between devices, local(): lax.all_to_all(expert_rows, 'expert', split_axis=0, concat_axis=0, tiled=...  13 us
  transfers between devices with their start and end apart: 4, of which 4 were waited for; matrix products, arithmetic and copies ran while one was open for 6% of the time, Pallas kernels for 0%

commit v1 on v0

--- a/solution.py
+++ b/solution.py
@@ -5,6 +5,14 @@
 
 
 def local(tokens, gate_train, up_train, down_train, routes, route_scores, live):
+
+    def field_do(device_axis, x0):
+        z_new = lax.all_to_all(
+            jnp.stack([x0 for _ in range(lax.axis_size(device_axis))]), device_axis, 0, 0
+        )
+        arr_out = jnp.concatenate(z_new, axis=1)
+        return arr_out
+
     local_experts = gate_train.shape[0]
     hidden_width = gate_train.shape[2]
     holders = lax.axis_size("expert")
@@ -34,7 +42,7 @@
     gate_up_local = jnp.concatenate([gate_train, up_train], axis=2).astype(jnp.bfloat16)
     down_local = down_train.astype(jnp.bfloat16)
     gate_up_w, down_w = (
-        lax.all_gather(gate_up_local, "group", axis=1, tiled=True),
+        field_do("group", gate_up_local),
         lax.all_gather(down_local, "group", axis=2, tiled=True),
     )
     gate_up = jnp.einsum("sjcd,jdf->sjcf", incoming, gate_up_w, preferred_element_type=jnp.float32)

time: 406 us -> 478 us (1.18)
  the two profiles are of different devices: /device:TPU:48 before, /device:TPU:56 now
where the time goes in v1:
time: 478 us; the launch traced here: 477 us
  waiting for transfers between devices  370 us (77%)
  starting transfers between devices  38.4 us (8%)
  local copies, waits for them, and re-layouts  32.3 us (7%)
  between operations  13.6 us (3%)
  other arithmetic  12.1 us (3%)
  matrix products  11.4 us (2%)
    all_to_all x1, waiting for transfers between devices, field_do(): lax.all_to_all(jnp.stack([x0 for _ in range(lax.axis_size(device_axis))])...  121 us
    all_to_all x1, waiting for transfers between devices, local(): lax.all_to_all(expert_rows, 'expert', split_axis=0, concat_axis=0, tiled=...  120 us
    all_to_all x1, waiting for transfers between devices, local(): lax.all_to_all(outgoing, 'expert', split_axis=0, concat_axis=0, tiled=True)  107 us
    all_gather x1, waiting for transfers between devices, local(): lax.all_gather(down_local, 'group', axis=2, tiled=True)  23 us
    all_to_all x1, starting transfers between devices, local(): lax.all_to_all(expert_rows, 'expert', split_axis=0, concat_axis=0, tiled=...  14.7 us
    all_to_all x1, starting transfers between devices, local(): lax.all_to_all(outgoing, 'expert', split_axis=0, concat_axis=0, tiled=True)  13.8 us
    all_to_all x1, starting transfers between devices, field_do(): lax.all_to_all(jnp.stack([x0 for _ in range(lax.axis_size(device_axis))])...  9.9 us
  transfers between devices with their start and end apart: 4, of which 4 were waited for; matrix products, arithmetic and copies ran while one was open for 6% of the time, Pallas kernels for 0%

profile of v1, /device:TPU:56, one launch (start us, length us, event | category | flops | bytes accessed | tf_op | source)
XLA Modules:
  0.0 477.5 jit_solution(17292416520306783433)
XLA Ops:
  6.5 0.0 copy-start
  6.5 1.0 convert.7
  7.5 0.9 convert.8
  8.5 3.5 stack.2
  12.0 0.0 copy-start.4
  12.0 0.0 copy-start.2
  12.0 9.9 %all-to-all-start = ((bf16[32,2,48,1024]{3,2,1,0:T(8,128)(2,1)}), bf16[32,2,48,1024]{3,2,1,0:T(8,128)(2,1)}, u32[]{:S(2)}, u32[]{:S(2)}) async-start(bf16[32,2,48,1024]{3,2,1,0:T(8,128)(2,1)} %stack.2), calls=%async_computation | async-start | bytes 12582912 | tf_op jit(solution)/shard_map/all_to_all | solution.py:10
  21.9 0.0 copy-done.4
  21.9 0.1 broadcast_in_dim.37.clone
  22.0 0.2 gt.41
  22.1 0.1 gt.40
  22.3 0.0 copy-done.2
  22.3 0.1 copy.28
  22.4 0.1 eq.29
  22.5 0.1 eq.25
  22.7 0.1 gt.39
  22.9 1.7 reduce-window.6
  24.6 0.3 slice_reduce_fusion
  24.9 0.1 copy.33
  25.0 0.1 mul.37
  25.2 0.1 fusion.14
  25.3 3.4 scatter_custom_fusion.1
  28.7 3.4 scatter_custom_fusion
  32.1 0.1 broadcast_in_dim.40
  32.2 0.0 copy-done
  32.2 2.9 gather_fusion
  35.2 1.6 broadcast_select_fusion
  36.8 0.0 copy-start.1
  36.8 120.6 %all-to-all-done = bf16[32,2,48,1024]{3,2,1,0:T(8,128)(2,1)} async-done(((bf16[32,2,48,1024]{3,2,1,0:T(8,128)(2,1)}), bf16[32,2,48,1024]{3,2,1,0:T(8,128)(2,1)}, u32[]{:S(2)}, u32[]{:S(2)}) %all-to-all-start) | async-done | bytes 6291488 | tf_op jit(solution)/shard_map/all_to_all | solution.py:10
  157.4 13.8 %all-to-all-start.1 = ((bf16[16,48,1536]{2,1,0:T(8,128)(2,1)}), bf16[16,48,1536]{2,1,0:T(8,128)(2,1)S(1)}, u32[]{:S(2)}, u32[]{:S(2)}) async-start(bf16[16,48,1536]{2,1,0:T(8,128)(2,1)} %broadcast_select_fusion), calls=%async_computation.1 | async-start | bytes 4718592 | tf_op jit(solution)/shard_map/all_to_all | solution.py:40
  171.2 0.0 all-gather.2.cloned.1.call-start
  171.2 0.0 copy-done.1
  171.2 0.7 convert_element_type.34
  171.9 0.0 all-gather.2.cloned.1.call-update
  171.9 6.7 %copy.26 = bf16[2,32,48,1024]{3,2,1,0:T(8,128)(2,1)} copy(bf16[2,32,48,1024]{3,2,0,1:T(8,128)(2,1)} %bitcast) | data formatting | bytes 12582912 | tf_op jit(solution)/shard_map/reshape | solution.py:13
  178.6 106.6 %all-to-all-done.1 = bf16[16,48,1536]{2,1,0:T(8,128)(2,1)S(1)} async-done(((bf16[16,48,1536]{2,1,0:T(8,128)(2,1)}), bf16[16,48,1536]{2,1,0:T(8,128)(2,1)S(1)}, u32[]{:S(2)}, u32[]{:S(2)}) %all-to-all-start.1) | async-done | bytes 2359328 | tf_op jit(solution)/shard_map/all_to_all | solution.py:40
  285.2 7.0 %fusion.6 = f32[16,2,24,1024]{3,2,0,1:T(8,128)} fusion(bf16[2,1536,1024,1]{2,1,3,0:T(8,128)(2,1)} %bitcast.45, bf16[16,2,24,1536]{3,2,1,0:T(8,128)(2,1)S(1)} %bitcast.46), kind=kOutput, calls=%fused_computation.11 | convolution fusion | flops 2415919104 | bytes 11796480 | tf_op jit(solution)/shard_map/sjcd,jdf->sjcf/dot_general | solution.py:48
  292.3 23.0 %all-gather.2.cloned.1.call-done = bf16[2,512,1536]{1,2,0:T(8,128)(2,1)} async-done(((bf16[2,512,48]{1,2,0:T(8,128)(2,1)}), bf16[2,512,1536]{1,2,0:T(8,128)(2,1)}) %all-gather.2.cloned.1.call-update) | async-done | bytes 3145744 | tf_op jit(solution)/shard_map/all_gather | solution.py:46
  315.2 4.3 fusion.1
  319.6 1.7 copy.35
  321.3 0.0 copy-start.3
  321.3 14.7 %all-to-all-start.2 = ((bf16[16,48,1536]{2,1,0:T(8,128)(2,1)}), bf16[16,48,1536]{2,1,0:T(8,128)(2,1)S(1)}, u32[]{:S(2)}, u32[]{:S(2)}) async-start(bf16[16,48,1536]{2,1,0:T(8,128)(2,1)} %bitcast.43), calls=%async_computation.2 | async-start | bytes 4718592 | tf_op jit(solution)/shard_map/all_to_all | solution.py:56
  335.9 0.2 lt.50
  336.1 0.1 copy.36
  336.2 0.0 copy-done.3
  336.2 0.1 copy.37
  336.4 119.5 %all-to-all-done.2 = bf16[16,48,1536]{2,1,0:T(8,128)(2,1)S(1)} async-done(((bf16[16,48,1536]{2,1,0:T(8,128)(2,1)}), bf16[16,48,1536]{2,1,0:T(8,128)(2,1)S(1)}, u32[]{:S(2)}, u32[]{:S(2)}) %all-to-all-start.2) | async-done | bytes 2359328 | tf_op jit(solution)/shard_map/all_to_all | solution.py:56
  455.9 3.9 gather_fusion.1
  459.8 5.0 %reshape.163 = f32[128,6,1536]{2,1,0:T(8,128)} reshape(bf16[768,1536]{1,0:T(8,128)(2,1)} %gather_fusion.1) | data formatting | bytes 7077888 | tf_op jit(solution)/shard_map/convert_element_type | solution.py:62
  464.7 5.9 %multiply_reduce_fusion = bf16[128,1536]{1,0:T(8,128)(2,1)} fusion(f32[128,6,1536]{2,1,0:T(8,128)} %reshape.163, f32[128,6]{1,0:T(8,128)S(1)} %copy.37), kind=kLoop, calls=%fused_computation.4 | loop fusion | flops 2162688 | bytes 5114880 | tf_op jit(solution)/shard_map/reduce_sum | solution.py:61
  (15 shorter events, 0.2 us)
Async XLA Ops:
  6.5 25.7 %copy-start = (bf16[128,1536]{1,0:T(8,128)(2,1)S(1)}, bf16[128,1536]{1,0:T(8,128)(2,1)}, u32[]{:S(2)}) copy-start(bf16[128,1536]{1,0:T(8,128)(2,1)} %param.7) | copy-start | bytes 1179652
  12.0 9.9 %copy-start.4 = (s32[128]{0:T(128)S(1)}, s32[128]{0:T(128)}, u32[]{:S(2)}) copy-start(s32[128]{0:T(128)} %param.13) | copy-start | bytes 1540
  12.0 10.3 %copy-start.2 = (s32[128,6]{0,1:T(8,128)S(1)}, s32[128,6]{0,1:T(8,128)}, u32[]{:S(2)}) copy-start(s32[128,6]{0,1:T(8,128)} %param.11) | copy-start | bytes 9220
  12.0 145.4 %all-to-all-start = ((bf16[32,2,48,1024]{3,2,1,0:T(8,128)(2,1)}), bf16[32,2,48,1024]{3,2,1,0:T(8,128)(2,1)}, u32[]{:S(2)}, u32[]{:S(2)}) async-start(bf16[32,2,48,1024]{3,2,1,0:T(8,128)(2,1)} %stack.2), calls=%async_computation | async-start | bytes 12582912 | tf_op jit(solution)/shard_map/all_to_all | solution.py:10
  36.8 134.4 %copy-start.1 = (f32[2,512,48]{1,2,0:T(8,128)S(1)}, f32[2,512,48]{1,2,0:T(8,128)}, u32[]{:S(2)}) copy-start(f32[2,512,48]{1,2,0:T(8,128)} %param.10) | copy-start | bytes 589828
  157.4 127.8 %all-to-all-start.1 = ((bf16[16,48,1536]{2,1,0:T(8,128)(2,1)}), bf16[16,48,1536]{2,1,0:T(8,128)(2,1)S(1)}, u32[]{:S(2)}, u32[]{:S(2)}) async-start(bf16[16,48,1536]{2,1,0:T(8,128)(2,1)} %broadcast_select_fusion), calls=%async_computation.1 | async-start | bytes 4718592 | tf_op jit(solution)/shard_map/all_to_all | solution.py:40
  171.2 144.1 %all-gather.2.cloned.1.call-start = ((), (), s32[]{:S(2)}) async-start(), calls=%async_computation.3 | async-start | bytes 3244032 | tf_op jit(solution)/shard_map/all_gather | solution.py:46
  321.3 14.9 %copy-start.3 = (f32[128,6]{0,1:T(8,128)S(1)}, f32[128,6]{0,1:T(8,128)}, u32[]{:S(2)}) copy-start(f32[128,6]{0,1:T(8,128)} %param.12) | copy-start | bytes 9220
  321.3 134.6 %all-to-all-start.2 = ((bf16[16,48,1536]{2,1,0:T(8,128)(2,1)}), bf16[16,48,1536]{2,1,0:T(8,128)(2,1)S(1)}, u32[]{:S(2)}, u32[]{:S(2)}) async-start(bf16[16,48,1536]{2,1,0:T(8,128)(2,1)} %bitcast.43), calls=%async_computation.2 | async-start | bytes 4718592 | tf_op jit(solution)/shard_map/all_to_all | solution.py:56
Sparse Core Ops, SparseCore 0:
  174.1 141.1 all-gather.1
